TPU v7x, 32 devices: a whole 2x2x4 slice. The times are simulated.
32 devices in a mesh: param: 4 (over y, core), ex: 8 (over z, x).
Axes of the slice: x: 2, y: 2, z: 4, core: 2. Of those that a mesh axis runs over, the one named last changes fastest.
Arguments:
- activations: bfloat16 [32, 128, 8192], P('ex', None, 'param'), may hold values from -6 to 6
- out_grads: bfloat16 [32, 128, 8192], P('ex', None, 'param'), may hold values from -6 to 6
- proj_in: bfloat16 [8192, 32], P('param'), may hold values from -0.0625 to 0.0625
- proj_out: bfloat16 [8192, 32], P('param'), may hold values from -0.0625 to 0.0625
- prior: float32 [1024, 1024], P('ex', 'param'), as said below
- probes: bfloat16 [512, 1024], P(('param', 'ex')), may hold values from -6 to 6
Outputs:
- scores: float32 [512, 32], P('param', 'ex')
Inputs may be any that keep to these rules, and one draw needn't show every extreme that they name: prior is symmetric positive definite with smallest eigenvalue at least 0.1.
All inputs are finite; a program needn't handle non-finite values.
Results may differ from a plain program's by a relative error of at most 0.0042.
Values may be sent and summed in bfloat16 or wider, within the bound.
No kernel may reach another device: no remote copies, remote signals or barrier semaphores. Data moves between devices by JAX's collectives and lax.ppermute only.
A program may use at most 64 MiB of HBM per device.

v0:
```python
import math
import jax
import jax.numpy as jnp
from jax import lax
from jax.sharding import PartitionSpec as P


def outer_terms(factors, in_width):
    first = factors[:, :in_width]
    second = factors[:, in_width:]
    product = jnp.einsum("eol,eil->eoi", second, first, precision=lax.Precision.HIGHEST)
    return product.reshape(product.shape[0], -1)


def solve_rows(lower_factor, rows):
    halfway = lax.linalg.triangular_solve(
        lower_factor, rows.astype(jnp.float32).T, left_side=True, lower=True
    )
    solved_t = lax.linalg.triangular_solve(
        lower_factor, halfway, left_side=True, lower=True, transpose_a=True
    )
    return solved_t.T.astype(jnp.bfloat16)


def per_device(activations, out_grads, proj_in, proj_out, prior, probes):
    tokens = activations.shape[1]
    in_width = proj_in.shape[1]
    factor_in = jnp.einsum("eld,dk->ekl", activations, proj_in, preferred_element_type=jnp.float32)
    factor_out = jnp.einsum("eld,dk->ekl", out_grads, proj_out, preferred_element_type=jnp.float32)
    factors = jnp.concatenate((factor_in, factor_out), axis=1)
    factors = lax.psum(factors, "param")
    summed = outer_terms(factors, in_width)
    features = (summed * (1.0 / math.sqrt(tokens))).astype(jnp.bfloat16)
    feat_dim = features.shape[1]
    block_width = feat_dim // lax.axis_size("param")
    column_start = lax.axis_index("param") * block_width
    train_count = features.shape[0] * lax.axis_size("ex")
    row_start = lax.axis_index("ex") * prior.shape[0]
    placed = lax.dynamic_update_slice(
        jnp.zeros((feat_dim, block_width), jnp.float32), prior, (row_start, jnp.int32(0))
    )
    columns = lax.dynamic_slice_in_dim(features, column_start, block_width, 1)
    kernel_block = lax.psum(
        placed
        + lax.dot_general(
            features, columns, (((0,), (0,)), ((), ())), preferred_element_type=jnp.float32
        )
        / train_count,
        "ex",
    )
    kernel = lax.all_gather(kernel_block, "param", axis=1, tiled=True)
    lower_factor = jnp.linalg.cholesky(kernel)
    inverse_root = 1.0 / math.sqrt(feat_dim)
    solved = solve_rows(lower_factor, features)
    return (
        jnp.dot(
            lax.all_gather(probes, "ex", axis=0, tiled=True),
            solved.T,
            preferred_element_type=jnp.float32,
        )
        * inverse_root
    )


def solution(mesh):
    return jax.shard_map(
        per_device,
        mesh=mesh,
        in_specs=(
            P("ex", None, "param"),
            P("ex", None, "param"),
            P("param", None),
            P("param", None),
            P("ex", "param"),
            P(("param", "ex"), None),
        ),
        out_specs=P("param", "ex"),
        check_vma=False,
    )
```

profile of v0, /device:TPU:0, one launch (start us, length us, event | category | flops | bytes accessed | tf_op | source)
XLA Modules:
  0.0 520.8 jit_solution(16283190189120157218)
XLA Ops:
  13.0 34.1 %all-reduce.4.cloned.1.call-done = f32[4,64,128]{2,1,0:T(8,128)} async-done(((f32[4,64,128]{2,1,0:T(8,128)}), f32[4,64,128]{2,1,0:T(8,128)}) %all-reduce.4.cloned.1.call-update) | async-done | bytes 131088 | tf_op jit(solution)/shard_map/psum | solution.py:31
  49.8 79.2 %all-reduce.6.cloned.1.call-done = f32[1024,256]{0,1:T(8,128)} async-done(((f32[1024,256]{0,1:T(8,128)}), f32[1024,256]{0,1:T(8,128)}) %all-reduce.6.cloned.1.call-update) | async-done | bytes 1048592 | tf_op jit(solution)/shard_map/psum | solution.py:43
  129.1 30.8 %all_gather.7 = bf16[128,1024]{1,0:T(8,128)(2,1)S(1)} all-gather(bf16[16,1024]{1,0:T(8,128)(2,1)S(1)} %copy-done.4), channel_id=1, replica_groups=mesh['param'=4,'ex'=8] {'ex'}, dimensions={0}, use_global_device_ids=true | all-gather | bytes 294912 | tf_op jit(solution)/shard_map/all_gather | solution.py:57
  159.9 4.8 all-gather.2.cloned.1.call-done
  164.7 5.6 %copy.9 = f32[1024,1024]{1,0:T(8,128)} copy(f32[1024,1024]{0,1:T(8,128)} %all-gather.2.cloned.1.call-done) | data formatting | bytes 8388608 | tf_op jit(solution)/shard_map/all_gather | solution.py:51
  170.3 4.4 fusion
  176.7 11.7 %cholesky.223 = f32[128,128]{1,0:T(8,128)S(1)} custom-call(f32[128,128]{1,0:T(8,128)S(1)} %cholesky.580), custom_call_target="Cholesky" | custom-call | tf_op jit(solution)/shard_map/jit(cholesky)/cholesky | solution.py:52
  188.5 9.8 %custom-call.64 = f32[1,128,128]{1,2,0:T(8,128)S(1)} custom-call(f32[1,128,128]{2,1,0:T(8,128)S(1)} %get-tuple-element.44), custom_call_target="InvertDiagBlocksLowerTriangular" | custom-call | tf_op jit(solution)/shard_map/jit(cholesky)/cholesky | solution.py:52
  204.7 12.2 %cholesky.244 = f32[128,128]{1,0:T(8,128)S(1)} custom-call(f32[128,128]{1,0:T(8,128)S(1)} %cholesky.584), custom_call_target="Cholesky" | custom-call | tf_op jit(solution)/shard_map/jit(cholesky)/cholesky | solution.py:52
  217.6 9.8 %custom-call.65 = f32[1,128,128]{1,2,0:T(8,128)S(1)} custom-call(f32[1,128,128]{2,1,0:T(8,128)S(1)} %get-tuple-element.41), custom_call_target="InvertDiagBlocksLowerTriangular" | custom-call | tf_op jit(solution)/shard_map/jit(cholesky)/cholesky | solution.py:52
  230.7 11.7 %cholesky.468 = f32[128,128]{1,0:T(8,128)S(1)} custom-call(f32[128,128]{1,0:T(8,128)S(1)} %cholesky.589), custom_call_target="Cholesky" | custom-call | tf_op jit(solution)/shard_map/jit(cholesky)/cholesky | solution.py:52
  243.7 9.8 %custom-call.66 = f32[1,128,128]{1,2,0:T(8,128)S(1)} custom-call(f32[1,128,128]{2,1,0:T(8,128)S(1)} %get-tuple-element.38), custom_call_target="InvertDiagBlocksLowerTriangular" | custom-call | tf_op jit(solution)/shard_map/jit(cholesky)/cholesky | solution.py:52
  257.1 11.8 %cholesky.487 = f32[128,128]{1,0:T(8,128)S(1)} custom-call(f32[128,128]{1,0:T(8,128)S(1)} %cholesky.594), custom_call_target="Cholesky" | custom-call | tf_op jit(solution)/shard_map/jit(cholesky)/cholesky | solution.py:52
  270.3 9.8 %custom-call.67 = f32[1,128,128]{1,2,0:T(8,128)S(1)} custom-call(f32[1,128,128]{2,1,0:T(8,128)S(1)} %get-tuple-element.35), custom_call_target="InvertDiagBlocksLowerTriangular" | custom-call | tf_op jit(solution)/shard_map/jit(cholesky)/cholesky | solution.py:52
  283.5 11.7 %cholesky.506 = f32[128,128]{1,0:T(8,128)S(1)} custom-call(f32[128,128]{1,0:T(8,128)S(1)} %cholesky.599), custom_call_target="Cholesky" | custom-call | tf_op jit(solution)/shard_map/jit(cholesky)/cholesky | solution.py:52
  296.5 10.0 %custom-call.68 = f32[1,128,128]{1,2,0:T(8,128)S(1)} custom-call(f32[1,128,128]{2,1,0:T(8,128)S(1)} %get-tuple-element.32), custom_call_target="InvertDiagBlocksLowerTriangular" | custom-call | tf_op jit(solution)/shard_map/jit(cholesky)/cholesky | solution.py:52
  309.8 11.7 %cholesky.526 = f32[128,128]{1,0:T(8,128)S(1)} custom-call(f32[128,128]{1,0:T(8,128)S(1)} %cholesky.604), custom_call_target="Cholesky" | custom-call | tf_op jit(solution)/shard_map/jit(cholesky)/cholesky | solution.py:52
  322.8 9.8 %custom-call.69 = f32[1,128,128]{1,2,0:T(8,128)S(1)} custom-call(f32[1,128,128]{2,1,0:T(8,128)S(1)} %get-tuple-element.29), custom_call_target="InvertDiagBlocksLowerTriangular" | custom-call | tf_op jit(solution)/shard_map/jit(cholesky)/cholesky | solution.py:52
  335.6 12.1 %cholesky.546 = f32[128,128]{1,0:T(8,128)S(1)} custom-call(f32[128,128]{1,0:T(8,128)S(1)} %cholesky.609), custom_call_target="Cholesky" | custom-call | tf_op jit(solution)/shard_map/jit(cholesky)/cholesky | solution.py:52
  349.0 9.8 %custom-call.70 = f32[1,128,128]{1,2,0:T(8,128)S(1)} custom-call(f32[1,128,128]{2,1,0:T(8,128)S(1)} %get-tuple-element.26), custom_call_target="InvertDiagBlocksLowerTriangular" | custom-call | tf_op jit(solution)/shard_map/jit(cholesky)/cholesky | solution.py:52
  361.5 11.7 %cholesky.564 = f32[128,128]{1,0:T(8,128)S(1)} custom-call(f32[128,128]{1,0:T(8,128)S(1)} %convolution_subtract_fusion.6), custom_call_target="Cholesky" | custom-call | tf_op jit(solution)/shard_map/jit(cholesky)/cholesky | solution.py:52
  380.2 4.8 select_select_fusion
  385.0 27.6 %while.1 = (s32[]{:T(128)}, f32[1024,1024]{1,0:T(8,128)}, s32[8,2]{0,1:T(2,128)S(1)}, f32[8,128,128]{2,1,0:T(8,128)}, s32[]{:T(128)}) while((s32[]{:T(128)}, f32[1024,1024]{1,0:T(8,128)}, s32[8,2]{0,1:T(2,128)S(1)}, f32[8,128,128]{2,1,0:T(8,128)}, s32[]{:T(128)}) %tuple.57), condition=%wide.while_cond, body=%wide.while_body.sunk | while | flops 2 | bytes 132705 | solution.py:19
  385.6 2.9 bitcast_dynamic-update-slice_fusion.2
  389.1 2.8 bitcast_dynamic-update-slice_fusion.2
  392.5 2.8 bitcast_dynamic-update-slice_fusion.2
  396.0 2.8 bitcast_dynamic-update-slice_fusion.2
  399.5 2.8 bitcast_dynamic-update-slice_fusion.2
  402.9 2.8 bitcast_dynamic-update-slice_fusion.2
  406.4 2.8 bitcast_dynamic-update-slice_fusion.2
  409.9 2.8 bitcast_dynamic-update-slice_fusion.2
  412.6 79.6 %custom-call.71 = f32[8,128,128]{1,2,0:T(8,128)S(1)} custom-call(f32[8,128,128]{2,1,0:T(8,128)} %get-tuple-element.12), custom_call_target="InvertDiagBlocksLowerTriangular" | custom-call | tf_op jit(solution)/shard_map/triangular_solve | solution.py:19
  (134 shorter events, 72.6 us)
Async XLA Ops:
  6.5 1.6 copy-start
  6.5 6.4 %copy-start.3 = (f32[128,256]{1,0:T(8,128)S(1)}, f32[128,256]{1,0:T(8,128)}, u32[]{:S(2)}) copy-start(f32[128,256]{1,0:T(8,128)} %param.10) | copy-start | bytes 393220
  6.5 122.5 %copy-start.4 = (bf16[16,1024]{1,0:T(8,128)(2,1)S(1)}, bf16[16,1024]{1,0:T(8,128)(2,1)}, u32[]{:S(2)}) copy-start(bf16[16,1024]{1,0:T(8,128)(2,1)} %param.11) | copy-start | bytes 98308
  6.5 40.6 %all-reduce.4.cloned.1.call-start = ((), (), s32[]{:S(2)}) async-start(), calls=%async_computation | async-start | bytes 262144 | tf_op jit(solution)/shard_map/psum | solution.py:31
  12.9 116.2 %all-reduce.6.cloned.1.call-start = ((), (), s32[]{:S(2)}) async-start(), calls=%async_computation.1 | async-start | bytes 2097152 | tf_op jit(solution)/shard_map/psum | solution.py:43
  48.7 1.0 copy-start.2
  49.7 115.0 %all-gather.2.cloned.1.call-start = ((), (), s32[]{:S(2)}) async-start(), calls=%async_computation.2 | async-start | bytes 5242880 | tf_op jit(solution)/shard_map/all_gather | solution.py:51
  174.8 1.9 copy-start.1
Sparse Core Ops, SparseCore 0:
  13.0 34.0 all-reduce.3
  51.0 77.9 all-reduce.5
  130.6 34.0 all-gather.1
where the time goes:
time: 525 us; the launch traced here: 521 us
  other arithmetic  262 us (50%)
  waiting for transfers between devices  118 us (22%)
  matrix products  50 us (10%)
  local copies, waits for them, and re-layouts  40.7 us (8%)
  blocking collectives  30.8 us (6%)
  between operations  18.6 us (4%)
    another operation x30, other arithmetic, per_device(): lower_factor = jnp.linalg.cholesky(kernel)  173 us
    another operation x4, other arithmetic, solve_rows(): lax.linalg.triangular_solve(lower_factor, halfway, left_side=True, lower=...  84.4 us
    psum x1, waiting for transfers between devices, per_device(): lax.psum(placed + lax.dot_general(features, columns, (((0,), (0,)), ((),...  79.2 us
    psum x1, waiting for transfers between devices, per_device(): factors = lax.psum(factors, 'param')  34.1 us
    all_gather x1, blocking collectives, per_device(): lax.all_gather(probes, 'ex', axis=0, tiled=True)  30.8 us
    another operation x24, local copies, waits for them, and re-layouts  27.6 us
    another operation x14, matrix products, per_device(): lower_factor = jnp.linalg.cholesky(kernel)  23.1 us
    another operation x15, matrix products, solve_rows(): lax.linalg.triangular_solve(lower_factor, rows.astype(jnp.float32).T, lef...  10.6 us
  transfers between devices with their start and end apart: 3, of which 3 were waited for; matrix products, arithmetic and copies ran while one was open for 0% of the time, Pallas kernels for 0%

commit v1 on v0

--- a/solution.py
+++ b/solution.py
@@ -28,7 +28,7 @@
     factor_in = jnp.einsum("eld,dk->ekl", activations, proj_in, preferred_element_type=jnp.float32)
     factor_out = jnp.einsum("eld,dk->ekl", out_grads, proj_out, preferred_element_type=jnp.float32)
     factors = jnp.concatenate((factor_in, factor_out), axis=1)
-    factors = lax.psum(factors, "param")
+    factors = jnp.sum(lax.all_gather(factors, "param"), axis=0)
     summed = outer_terms(factors, in_width)
     features = (summed * (1.0 / math.sqrt(tokens))).astype(jnp.bfloat16)
     feat_dim = features.shape[1]

time: 525 us -> 498 us (0.949)
  waiting for transfers between devices: 118 us -> 83.9 us
  blocking collectives: 30.8 us -> 39.4 us
    psum x1 -> x0, waiting for transfers between devices: 34.1 us -> none  [per_device(): factors = lax.psum(factors, 'param')]
    all_gather x0 -> x1, blocking collectives: none -> 8.65 us  [per_device(): factors = jnp.sum(lax.all_gather(factors, 'param'), axis=0)]
  transfers between devices with their start and end apart: 3 -> 2, of which waited for: 3 -> 2; matrix products, arithmetic and copies ran while one was open for 0% -> 0% of each run, Pallas kernels for 0% -> 0%
where the time goes in v1:
time: 498 us; the launch traced here: 494 us
  other arithmetic  262 us (53%)
  waiting for transfers between devices  83.9 us (17%)
  matrix products  49.1 us (10%)
  local copies, waits for them, and re-layouts  40.7 us (8%)
  blocking collectives  39.4 us (8%)
  between operations  18.9 us (4%)
    another operation x30, other arithmetic, per_device(): lower_factor = jnp.linalg.cholesky(kernel)  173 us
    another operation x4, other arithmetic, solve_rows(): lax.linalg.triangular_solve(lower_factor, halfway, left_side=True, lower=...  84.4 us
    psum x1, waiting for transfers between devices, per_device(): lax.psum(placed + lax.dot_general(features, columns, (((0,), (0,)), ((),...  79 us
    all_gather x1, blocking collectives, per_device(): lax.all_gather(probes, 'ex', axis=0, tiled=True)  30.8 us
    another operation x24, local copies, waits for them, and re-layouts  27.6 us
    another operation x14, matrix products, per_device(): lower_factor = jnp.linalg.cholesky(kernel)  23.1 us
    another operation x15, matrix products, solve_rows(): lax.linalg.triangular_solve(lower_factor, rows.astype(jnp.float32).T, lef...  10.6 us
    another operation x15, matrix products, solve_rows(): lax.linalg.triangular_solve(lower_factor, halfway, left_side=True, lower=...  10.1 us
  transfers between devices with their start and end apart: 2, of which 2 were waited for; matrix products, arithmetic and copies ran while one was open for 0% of the time, Pallas kernels for 0%

profile of v1, /device:TPU:0, one launch (start us, length us, event | category | flops | bytes accessed | tf_op | source)
XLA Modules:
  0.0 494.0 jit_solution(5794084756020645)
XLA Ops:
  12.2 8.6 %all-gather = f32[16,64,128]{2,1,0:T(8,128)S(1)} all-gather(f32[4,64,128]{2,1,0:T(8,128)S(1)} %pad_maximum_fusion), channel_id=2, replica_groups=mesh['param'=4,'ex'=8] {'param'}, dimensions={0}, use_global_device_ids=true | all-gather | bytes 655360 | tf_op jit(solution)/shard_map/all_gather | solution.py:31
  22.8 79.0 %all-reduce.3.cloned.1.call-done = f32[1024,256]{0,1:T(8,128)} async-done(((f32[1024,256]{0,1:T(8,128)}), f32[1024,256]{0,1:T(8,128)}) %all-reduce.3.cloned.1.call-update) | async-done | bytes 1048592 | tf_op jit(solution)/shard_map/psum | solution.py:43
  101.8 30.8 %all_gather.15 = bf16[128,1024]{1,0:T(8,128)(2,1)S(1)} all-gather(bf16[16,1024]{1,0:T(8,128)(2,1)S(1)} %copy-done.4), channel_id=1, replica_groups=mesh['param'=4,'ex'=8] {'ex'}, dimensions={0}, use_global_device_ids=true | all-gather | bytes 294912 | tf_op jit(solution)/shard_map/all_gather | solution.py:57
  132.6 4.9 all-gather.3.cloned.1.call-done
  137.5 5.6 %copy.12 = f32[1024,1024]{1,0:T(8,128)} copy(f32[1024,1024]{0,1:T(8,128)} %all-gather.3.cloned.1.call-done) | data formatting | bytes 8388608 | tf_op jit(solution)/shard_map/all_gather | solution.py:51
  143.2 4.4 fusion
  149.5 11.7 %cholesky.223 = f32[128,128]{1,0:T(8,128)S(1)} custom-call(f32[128,128]{1,0:T(8,128)S(1)} %cholesky.580), custom_call_target="Cholesky" | custom-call | tf_op jit(solution)/shard_map/jit(cholesky)/cholesky | solution.py:52
  163.8 9.8 %custom-call.64 = f32[1,128,128]{1,2,0:T(8,128)S(1)} custom-call(f32[1,128,128]{2,1,0:T(8,128)S(1)} %get-tuple-element.44), custom_call_target="InvertDiagBlocksLowerTriangular" | custom-call | tf_op jit(solution)/shard_map/jit(cholesky)/cholesky | solution.py:52
  177.5 12.2 %cholesky.244 = f32[128,128]{1,0:T(8,128)S(1)} custom-call(f32[128,128]{1,0:T(8,128)S(1)} %cholesky.584), custom_call_target="Cholesky" | custom-call | tf_op jit(solution)/shard_map/jit(cholesky)/cholesky | solution.py:52
  190.4 9.8 %custom-call.65 = f32[1,128,128]{1,2,0:T(8,128)S(1)} custom-call(f32[1,128,128]{2,1,0:T(8,128)S(1)} %get-tuple-element.41), custom_call_target="InvertDiagBlocksLowerTriangular" | custom-call | tf_op jit(solution)/shard_map/jit(cholesky)/cholesky | solution.py:52
  203.6 11.7 %cholesky.468 = f32[128,128]{1,0:T(8,128)S(1)} custom-call(f32[128,128]{1,0:T(8,128)S(1)} %cholesky.589), custom_call_target="Cholesky" | custom-call | tf_op jit(solution)/shard_map/jit(cholesky)/cholesky | solution.py:52
  216.6 9.8 %custom-call.66 = f32[1,128,128]{1,2,0:T(8,128)S(1)} custom-call(f32[1,128,128]{2,1,0:T(8,128)S(1)} %get-tuple-element.38), custom_call_target="InvertDiagBlocksLowerTriangular" | custom-call | tf_op jit(solution)/shard_map/jit(cholesky)/cholesky | solution.py:52
  229.9 11.8 %cholesky.487 = f32[128,128]{1,0:T(8,128)S(1)} custom-call(f32[128,128]{1,0:T(8,128)S(1)} %cholesky.594), custom_call_target="Cholesky" | custom-call | tf_op jit(solution)/shard_map/jit(cholesky)/cholesky | solution.py:52
  243.1 9.8 %custom-call.67 = f32[1,128,128]{1,2,0:T(8,128)S(1)} custom-call(f32[1,128,128]{2,1,0:T(8,128)S(1)} %get-tuple-element.35), custom_call_target="InvertDiagBlocksLowerTriangular" | custom-call | tf_op jit(solution)/shard_map/jit(cholesky)/cholesky | solution.py:52
  256.4 11.7 %cholesky.506 = f32[128,128]{1,0:T(8,128)S(1)} custom-call(f32[128,128]{1,0:T(8,128)S(1)} %cholesky.599), custom_call_target="Cholesky" | custom-call | tf_op jit(solution)/shard_map/jit(cholesky)/cholesky | solution.py:52
  269.4 10.0 %custom-call.68 = f32[1,128,128]{1,2,0:T(8,128)S(1)} custom-call(f32[1,128,128]{2,1,0:T(8,128)S(1)} %get-tuple-element.32), custom_call_target="InvertDiagBlocksLowerTriangular" | custom-call | tf_op jit(solution)/shard_map/jit(cholesky)/cholesky | solution.py:52
  282.7 11.7 %cholesky.526 = f32[128,128]{1,0:T(8,128)S(1)} custom-call(f32[128,128]{1,0:T(8,128)S(1)} %cholesky.604), custom_call_target="Cholesky" | custom-call | tf_op jit(solution)/shard_map/jit(cholesky)/cholesky | solution.py:52
  295.7 9.8 %custom-call.69 = f32[1,128,128]{1,2,0:T(8,128)S(1)} custom-call(f32[1,128,128]{2,1,0:T(8,128)S(1)} %get-tuple-element.29), custom_call_target="InvertDiagBlocksLowerTriangular" | custom-call | tf_op jit(solution)/shard_map/jit(cholesky)/cholesky | solution.py:52
  308.5 12.1 %cholesky.546 = f32[128,128]{1,0:T(8,128)S(1)} custom-call(f32[128,128]{1,0:T(8,128)S(1)} %cholesky.609), custom_call_target="Cholesky" | custom-call | tf_op jit(solution)/shard_map/jit(cholesky)/cholesky | solution.py:52
  321.9 9.8 %custom-call.70 = f32[1,128,128]{1,2,0:T(8,128)S(1)} custom-call(f32[1,128,128]{2,1,0:T(8,128)S(1)} %get-tuple-element.26), custom_call_target="InvertDiagBlocksLowerTriangular" | custom-call | tf_op jit(solution)/shard_map/jit(cholesky)/cholesky | solution.py:52
  334.3 11.7 %cholesky.564 = f32[128,128]{1,0:T(8,128)S(1)} custom-call(f32[128,128]{1,0:T(8,128)S(1)} %convolution_subtract_fusion.6), custom_call_target="Cholesky" | custom-call | tf_op jit(solution)/shard_map/jit(cholesky)/cholesky | solution.py:52
  353.0 4.8 select_select_fusion
  357.8 27.6 %while.1 = (s32[]{:T(128)}, f32[1024,1024]{1,0:T(8,128)}, s32[8,2]{0,1:T(2,128)S(1)}, f32[8,128,128]{2,1,0:T(8,128)}, s32[]{:T(128)}) while((s32[]{:T(128)}, f32[1024,1024]{1,0:T(8,128)}, s32[8,2]{0,1:T(2,128)S(1)}, f32[8,128,128]{2,1,0:T(8,128)}, s32[]{:T(128)}) %tuple.57), condition=%wide.while_cond, body=%wide.while_body.sunk | while | flops 2 | bytes 132705 | solution.py:19
  358.4 2.9 bitcast_dynamic-update-slice_fusion.2
  361.9 2.8 bitcast_dynamic-update-slice_fusion.2
  365.4 2.8 bitcast_dynamic-update-slice_fusion.2
  368.8 2.8 bitcast_dynamic-update-slice_fusion.2
  372.3 2.8 bitcast_dynamic-update-slice_fusion.2
  375.8 2.8 bitcast_dynamic-update-slice_fusion.2
  379.2 2.8 bitcast_dynamic-update-slice_fusion.2
  382.7 2.8 bitcast_dynamic-update-slice_fusion.2
  385.5 79.6 %custom-call.71 = f32[8,128,128]{1,2,0:T(8,128)S(1)} custom-call(f32[8,128,128]{2,1,0:T(8,128)} %get-tuple-element.12), custom_call_target="InvertDiagBlocksLowerTriangular" | custom-call | tf_op jit(solution)/shard_map/triangular_solve | solution.py:19
  (133 shorter events, 71.1 us)
Async XLA Ops:
  6.5 1.6 copy-start
  6.5 14.7 %copy-start.3 = (f32[128,256]{1,0:T(8,128)S(1)}, f32[128,256]{1,0:T(8,128)}, u32[]{:S(2)}) copy-start(f32[128,256]{1,0:T(8,128)} %param.10) | copy-start | bytes 393220
  6.5 95.3 %all-reduce.3.cloned.1.call-start = ((), (), s32[]{:S(2)}) async-start(), calls=%async_computation | async-start | bytes 2097152 | tf_op jit(solution)/shard_map/psum | solution.py:43
  9.8 92.1 %copy-start.4 = (bf16[16,1024]{1,0:T(8,128)(2,1)S(1)}, bf16[16,1024]{1,0:T(8,128)(2,1)}, u32[]{:S(2)}) copy-start(bf16[16,1024]{1,0:T(8,128)(2,1)} %param.11) | copy-start | bytes 98308
  21.7 1.0 copy-start.2
  22.7 114.8 %all-gather.3.cloned.1.call-start = ((), (), s32[]{:S(2)}) async-start(), calls=%async_computation.1 | async-start | bytes 5242880 | tf_op jit(solution)/shard_map/all_gather | solution.py:51
  147.6 1.9 copy-start.1
Sparse Core Ops, SparseCore 0:
  22.9 78.8 all-reduce.2
  103.4 34.0 all-gather.2
